TPU v7x, 32 devices: a whole 2x2x4 slice. The times are simulated.
32 devices in a mesh: pw: 8 (over z, y), band: 4 (over x, core).
Axes of the slice: x: 2, y: 2, z: 4, core: 2. Of those that a mesh axis runs over, the one named last changes fastest.
Arguments:
- psi_block: float32 [2, 8, 256, 128], P(None, 'band', 'pw'), may hold values from -6 to 6
- psi_all: bfloat16 [2, 1024, 256, 128], P(None, 'band', 'pw'), may hold values from -0.0234375 to 0.0234375
- potential: float32 [128, 128, 128], P('pw'), may hold values from -8 to 8
- stick_col: int32 [256], replicated, may hold values from 0 to 16383, as said below
Outputs:
- intersection: float32 [2, 8, 1024], P(None, 'pw', 'band')
- hpsi: float32 [2, 8, 256, 128], P(None, 'band', 'pw')
Inputs may be any that keep to these rules, and one draw needn't show every extreme that they name: `stick_col`: distinct columns of the 128 x 128 plane; column 0 and column 16383 are always among them.
All inputs are finite; a program needn't handle non-finite values.
Results may differ from a plain program's by a relative error of at most 0.0029.
Values may be sent and summed in bfloat16 or wider, within the bound.
No kernel may reach another device: no remote copies, remote signals or barrier semaphores. Data moves between devices by JAX's collectives and lax.ppermute only.
A program may use at most 64 MiB of HBM per device.

v0:
```python
import math
import jax
import numpy as np
import jax.numpy as jnp
from jax import lax
from jax.sharding import PartitionSpec as P


def frequency(index, size):
    return jnp.where(index < size // 2, index, index - size)


def kinetic_table(columns, grid_size):
    col_x = frequency(columns // grid_size, grid_size).astype(jnp.float32)
    col_y = frequency(columns % grid_size, grid_size).astype(jnp.float32)
    along = frequency(jnp.arange(grid_size, dtype=jnp.int32), grid_size).astype(jnp.float32)
    plane = col_x * col_x + col_y * col_y
    return 4.0 * (plane[:, None] + along[None, :] * along[None, :]) / float(grid_size * grid_size)


def dft_table(grid_size, sign):
    indices = np.arange(grid_size)
    products = indices[:, None] * indices[None, :] % grid_size
    angles = 2.0 * np.pi / grid_size * products
    cosine = np.cos(angles)
    sine = sign * np.sin(angles)
    table = np.stack([np.stack([cosine, -sine]), np.stack([sine, cosine])])
    return jnp.asarray(table.astype(np.float32))


def plane_tables(stick_col, grid_size):
    grid_iota = jnp.arange(grid_size, dtype=jnp.int32)
    col_x = stick_col // grid_size
    col_y = stick_col % grid_size
    phase_angles = (
        2.0
        * math.pi
        / grid_size
        * (grid_iota[:, None] * col_x[None, :] % grid_size).astype(jnp.float32)
    )
    place_cols = (col_y[:, None] == grid_iota[None, :]).astype(jnp.float32)
    pick_cols = (grid_iota[:, None] == col_y[None, :]).astype(jnp.float32)
    return (jnp.cos(phase_angles), jnp.sin(phase_angles), place_cols, pick_cols)


def mult(left, right):
    return jnp.dot(left, right, precision=lax.Precision.HIGH, preferred_element_type=jnp.float32)


def plane_phase(amp, pot, tables, grid_size):
    phase_cos, phase_sin, place_cols, pick_cols = tables
    inverse = dft_table(grid_size, 1.0)
    cosine = inverse[0, 0]
    sine = inverse[1, 0]
    scaled_pot = (pot / float(grid_size**3))[None]
    val_re = amp[0][:, :, None, :]
    val_im = amp[1][:, :, None, :]
    spread_re = val_re * phase_cos - val_im * phase_sin
    spread_im = val_re * phase_sin + val_im * phase_cos
    rows_re = mult(spread_re, place_cols)
    rows_im = mult(spread_im, place_cols)
    shared = mult(rows_re + rows_im, cosine)
    wave_re = (shared - mult(rows_im, cosine + sine)) * scaled_pot
    wave_im = (shared + mult(rows_re, sine - cosine)) * scaled_pot
    shared = mult(wave_re + wave_im, cosine)
    back_re = shared - mult(wave_im, cosine - sine)
    back_im = shared - mult(wave_re, sine + cosine)
    sel_re = mult(back_re, pick_cols)
    sel_im = mult(back_im, pick_cols)
    picked_re = jnp.sum(sel_re * phase_cos + sel_im * phase_sin, axis=2)
    picked_im = jnp.sum(sel_im * phase_cos - sel_re * phase_sin, axis=2)
    return jnp.stack([picked_re, picked_im])


def intersect(lowered, psi_all, pw_count):
    turned = jnp.stack([-lowered[1], lowered[0]])
    both = jnp.concatenate([lowered, turned], axis=1)
    dims = (((2, 3), (2, 3)), ((0,), (0,)))
    width = psi_all.shape[1] // 4
    partial_value = jnp.concatenate(
        [
            jnp.sum(
                lax.dot_general(
                    both,
                    psi_all[:, k * width : (k + 1) * width],
                    dims,
                    preferred_element_type=jnp.float32,
                ),
                axis=0,
            )
            for k in range(4)
        ],
        axis=-1,
    )
    partial_value = partial_value.reshape(2, lowered.shape[1], partial_value.shape[-1])
    rows_dev = partial_value.shape[1] // pw_count
    pieces = partial_value.reshape(2, pw_count, rows_dev, partial_value.shape[-1])
    pieces = lax.all_to_all(pieces, "pw", split_axis=1, concat_axis=1, tiled=True)
    return jnp.sum(pieces, axis=1)


def per_device_rows(psi_block, psi_all, potential, stick_col):
    sticks_dev = psi_block.shape[2]
    grid_size = psi_block.shape[3]
    fast = lax.Precision.HIGH
    rank = lax.axis_index("pw")
    pw_count = lax.axis_size("pw")
    planes = potential.shape[0]
    my_columns = lax.dynamic_slice_in_dim(stick_col, rank * sticks_dev, sticks_dev)
    kinetic = kinetic_table(my_columns, grid_size)
    inverse = dft_table(grid_size, 1.0)
    forward = dft_table(grid_size, -1.0)
    tables = plane_tables(stick_col, grid_size)
    parts = []
    for band in range(psi_block.shape[1]):
        coeffs = psi_block[:, band : band + 1]
        z_lines = jnp.einsum("dczk,cbsk->zdbs", inverse, coeffs, precision=fast)
        received = lax.all_to_all(z_lines, "pw", split_axis=0, concat_axis=0, tiled=True)
        lanes = received.shape[1:]
        received = received.reshape((pw_count, planes) + lanes)
        amp = jnp.transpose(received, (2, 3, 1, 0, 4)).reshape(
            lanes[0], lanes[1], planes, pw_count * sticks_dev
        )
        picked = plane_phase(amp, potential, tables, grid_size)
        outgoing = picked.reshape(lanes[0], lanes[1], planes, pw_count, sticks_dev)
        outgoing = jnp.transpose(outgoing, (3, 2, 0, 1, 4)).reshape((pw_count * planes,) + lanes)
        sticks_back = lax.all_to_all(outgoing, "pw", split_axis=0, concat_axis=0, tiled=True)
        parts.append(jnp.einsum("dckz,zcbs->dbsk", forward, sticks_back, precision=fast))
    vpsi = jnp.concatenate(parts, axis=1)
    applied = kinetic[None, None] * psi_block + vpsi
    lowered = applied.astype(jnp.bfloat16)
    gathered = lax.all_gather(lowered, "band", axis=1, tiled=True)
    intersection = intersect(gathered, psi_all, pw_count)
    return (intersection, applied)


def per_device(psi_block, psi_all, potential, stick_col):
    return per_device_rows(psi_block, psi_all, potential, stick_col)


def solution(mesh):
    return jax.shard_map(
        per_device,
        mesh=mesh,
        in_specs=(
            P(None, "band", "pw", None),
            P(None, "band", "pw", None),
            P("pw", None, None),
            P(),
        ),
        out_specs=(P(None, "pw", "band"), P(None, "band", "pw", None)),
        check_vma=False,
    )
```

profile of v0, /device:TPU:0, one launch (start us, length us, event | category | flops | bytes accessed | tf_op | source)
XLA Modules:
  0.0 94.0 jit_solution(17449898297534052666)
XLA Ops:
  0.6 1.2 %convolution_bitcast_fusion.1 = f32[128,2,1,32]{0,3,1,2:T(8,128)S(1)} fusion(f32[2,2,128,128]{3,2,1,0:T(8,128)} %constant.89.clone, f32[2,2,32,128]{3,2,1,0:T(8,128)} %param.8), kind=kOutput, calls=%fused_computation.33 | convolution fusion | flops 12582912 | bytes 327680 | tf_op jit(solution)/shard_map/dczk,cbsk->zdbs/dot_general | solution.py:117
  2.0 0.8 reshape.302
  2.7 7.3 %all-to-all-start.2 = ((f32[8,1,1024]{2,1,0:T(1,128)}), f32[8,1,1024]{2,1,0:T(1,128)S(1)}, u32[]{:S(2)}, u32[]{:S(2)}) async-start(f32[8,1,1024]{2,1,0:T(1,128)} %reshape.302), calls=%async_computation.2 | async-start | bytes 65536 | tf_op jit(solution)/shard_map/all_to_all | solution.py:118
  10.0 1.2 %convolution_bitcast_fusion.3 = f32[128,2,1,32]{0,3,1,2:T(8,128)S(1)} fusion(f32[2,2,128,128]{3,2,1,0:T(8,128)} %constant.89.clone, f32[2,2,32,128]{3,2,1,0:T(8,128)} %param.8), kind=kOutput, calls=%fused_computation.35 | convolution fusion | flops 12582912 | bytes 327680 | tf_op jit(solution)/shard_map/dczk,cbsk->zdbs/dot_general | solution.py:117
  11.2 0.7 and_select_fusion
  12.6 0.8 reshape.300
  13.4 4.1 %fusion.88 = (bf16[2,64,32,128]{3,2,1,0:T(8,128)(2,1)}, bf16[2,64,32,128]{3,2,1,0:T(8,128)(2,1)}, bf16[2,64,32,128]{3,2,1,0:T(8,128)(2,1)}, bf16[2,64,32,128]{3,2,1,0:T(8,128)(2,1)S(1)}) fusion(bf16[2,256,32,128]{3,2,1,0:T(8,128)(2,1)} %param.9), kind=kLoop, calls=%fused_computation.129 | loop fusion | bytes 8388608 | tf_op jit(solution)/shard_map/slice | solution.py:85
  17.6 6.0 %all-to-all-start = ((f32[8,1,1024]{2,1,0:T(1,128)}), f32[8,1,1024]{2,1,0:T(1,128)S(1)}, u32[]{:S(2)}, u32[]{:S(2)}) async-start(f32[8,1,1024]{2,1,0:T(1,128)} %reshape.300), calls=%async_computation | async-start | bytes 65536 | tf_op jit(solution)/shard_map/all_to_all | solution.py:118
  24.1 0.7 reduce.10
  25.3 0.8 fusion
  26.1 0.8 fusion.4
  26.9 3.4 %all-to-all-done = f32[8,1,1024]{2,1,0:T(1,128)S(1)} async-done(((f32[8,1,1024]{2,1,0:T(1,128)}), f32[8,1,1024]{2,1,0:T(1,128)S(1)}, u32[]{:S(2)}, u32[]{:S(2)}) %all-to-all-start) | async-done | bytes 32800 | tf_op jit(solution)/shard_map/all_to_all | solution.py:118
  30.3 0.7 reduce.9
  31.5 1.7 %fusion.12 = f32[16,128,128]{2,1,0:T(8,128)S(1)} fusion(f32[128,256]{1,0:T(8,128)} %copy-done.9, f32[16,256]{1,0:T(8,128)S(1)} %mul.266, f32[128,256]{1,0:T(8,128)S(1)} %get-tuple-element.30, f32[16,256]{1,0:T(8,128)S(1)} %mul.257, s32[256]{0:T(256)S(1)} %get-tuple-element.28), kind=kOutput, calls=%fused_computation.16 | convolution fusion | flops 404258816 | bytes 1344512 | tf_op jit(solution)/shard_map/dot_general | solution.py:47
  33.2 1.7 %fusion.8 = f32[16,128,128]{2,1,0:T(8,128)S(1)} fusion(f32[128,256]{1,0:T(8,128)} %copy-done.9, f32[16,256]{1,0:T(8,128)S(1)} %mul.266, f32[128,256]{1,0:T(8,128)S(1)} %get-tuple-element.30, f32[16,256]{1,0:T(8,128)S(1)} %mul.257, s32[256]{0:T(256)S(1)} %get-tuple-element.28), kind=kOutput, calls=%fused_computation.12 | convolution fusion | flops 404258816 | bytes 1344512 | tf_op jit(solution)/shard_map/dot_general | solution.py:47
  35.5 0.6 copy-done
  36.1 0.6 fusion.16
  36.9 0.6 fusion.17
  38.1 0.6 fusion.18
  38.7 0.6 fusion.19
  39.8 0.6 convolution_subtract_fusion
  41.8 0.6 convolution_subtract_fusion.3
  42.4 0.6 convolution_subtract_fusion.4
  43.0 0.7 fusion.60
  43.7 0.7 fusion.62
  44.4 0.9 fusion.66
  45.3 1.7 %add_reduce_fusion.1 = (f32[16,256]{1,0:T(8,128)S(1)}, f32[16,256]{1,0:T(8,128)S(1)}, f32[16,256]{1,0:T(8,128)S(1)}, f32[16,256]{1,0:T(8,128)S(1)}) fusion(f32[16,128,256]{2,1,0:T(8,128)S(1)} %fusion.66, f32[128,256]{1,0:T(8,128)S(1)} %copy-done.10, f32[128,256]{1,0:T(8,128)S(1)} %get-tuple-element.30, f32[16,128,256]{2,1,0:T(8,128)S(1)} %fusion.62, ...), kind=kOutput, calls=%fused_computation.11 | convolution fusion | flops 411058176 | bytes 7668736 | tf_op jit(solution)/shard_map/dot_general | solution.py:47
  47.3 0.8 reshape.306
  48.1 3.3 %all-to-all-start.1 = ((f32[8,1,1024]{2,1,0:T(1,128)}), f32[8,1,1024]{2,1,0:T(1,128)S(1)}, u32[]{:S(2)}, u32[]{:S(2)}) async-start(f32[8,1,1024]{2,1,0:T(1,128)} %reshape.306), calls=%async_computation.1 | async-start | bytes 65536 | tf_op jit(solution)/shard_map/all_to_all | solution.py:127
  51.8 0.8 reshape.304
  52.5 5.5 %all-to-all-done.1 = f32[8,1,1024]{2,1,0:T(1,128)S(1)} async-done(((f32[8,1,1024]{2,1,0:T(1,128)}), f32[8,1,1024]{2,1,0:T(1,128)S(1)}, u32[]{:S(2)}, u32[]{:S(2)}) %all-to-all-start.1) | async-done | bytes 32800 | tf_op jit(solution)/shard_map/all_to_all | solution.py:127
  58.1 4.0 %all-to-all-start.3 = ((f32[8,1,1024]{2,1,0:T(1,128)}), f32[8,1,1024]{2,1,0:T(1,128)}, u32[]{:S(2)}, u32[]{:S(2)}) async-start(f32[8,1,1024]{2,1,0:T(1,128)} %reshape.304), calls=%async_computation.3 | async-start | bytes 65536 | tf_op jit(solution)/shard_map/all_to_all | solution.py:127
  62.1 1.4 %reduce.12 = f32[8,1024]{1,0:T(8,128)} reduce(f32[8,1,1024]{2,1,0:T(1,128)S(1)} %all-to-all-done.1, f32[]{:T(128)} %broadcast.248), dimensions={1}, to_apply=%all_to_all.16.reduce_sub_computation | reduce | bytes 65540 | tf_op jit(solution)/shard_map/all_to_all | solution.py:127
  63.5 0.9 reshape.307
  64.4 0.7 copy.74
  65.1 3.6 %all-to-all-done.3 = f32[8,1,1024]{2,1,0:T(1,128)} async-done(((f32[8,1,1024]{2,1,0:T(1,128)}), f32[8,1,1024]{2,1,0:T(1,128)}, u32[]{:S(2)}, u32[]{:S(2)}) %all-to-all-start.3) | async-done | bytes 32800 | tf_op jit(solution)/shard_map/all_to_all | solution.py:127
  68.7 2.1 %reduce.11 = f32[8,1024]{1,0:T(8,128)} reduce(f32[8,1,1024]{2,1,0:T(1,128)} %all-to-all-done.3, f32[]{:T(128)} %broadcast.248), dimensions={1}, to_apply=%all_to_all.18.reduce_sub_computation | reduce | bytes 65540 | tf_op jit(solution)/shard_map/all_to_all | solution.py:127
  70.8 0.9 reshape.305
  71.8 0.7 copy.82
  72.5 1.0 %convolution_bitcast_fusion.2 = f32[2,1,32,128]{3,2,0,1:T(8,128)S(1)} fusion(f32[2,2,128,128]{3,2,1,0:T(8,128)S(1)} %copy-done.3, f32[128,2,1,32]{0,3,1,2:T(8,128)} %copy.74), kind=kOutput, calls=%fused_computation.34 | convolution fusion | flops 12582912 | bytes 327680 | tf_op jit(solution)/shard_map/dckz,zcbs->dbsk/dot_general | solution.py:128
  73.5 1.0 %convolution_bitcast_fusion = f32[2,1,32,128]{3,2,0,1:T(8,128)S(1)} fusion(f32[2,2,128,128]{3,2,1,0:T(8,128)S(1)} %copy-done.3, f32[128,2,1,32]{0,3,1,2:T(8,128)} %copy.82), kind=kOutput, calls=%fused_computation.32 | convolution fusion | flops 12582912 | bytes 327680 | tf_op jit(solution)/shard_map/dckz,zcbs->dbsk/dot_general | solution.py:128
  74.5 0.9 fusion.87
  75.4 5.4 %all_gather.3 = bf16[2,8,32,128]{3,2,0,1:T(8,128)(2,1)S(1)} all-gather(bf16[2,2,32,128]{3,2,0,1:T(8,128)(2,1)S(1)} %get-tuple-element.16), channel_id=1, replica_groups=mesh['pw'=8,'band'=4] {'band'}, dimensions={1}, use_global_device_ids=true | all-gather | bytes 163840 | tf_op jit(solution)/shard_map/all_gather | solution.py:132
  83.0 0.6 copy.90
  83.6 3.3 %all-to-all-start.4 = ((f32[2,8,1,256]{3,0,2,1:T(2,128)}), f32[2,8,1,256]{3,0,2,1:T(2,128)S(1)}, u32[]{:S(2)}, u32[]{:S(2)}) async-start(f32[2,8,1,256]{3,0,2,1:T(2,128)} %copy.90), calls=%async_computation.4 | async-start | bytes 32768 | tf_op jit(solution)/shard_map/all_to_all | solution.py:98
  86.9 0.6 copy.91
  87.5 5.9 %all-to-all-done.4 = f32[2,8,1,256]{3,0,2,1:T(2,128)S(1)} async-done(((f32[2,8,1,256]{3,0,2,1:T(2,128)}), f32[2,8,1,256]{3,0,2,1:T(2,128)S(1)}, u32[]{:S(2)}, u32[]{:S(2)}) %all-to-all-start.4) | async-done | bytes 16416 | tf_op jit(solution)/shard_map/all_to_all | solution.py:98
  93.4 0.6 reduce_sum.56
  (68 shorter events, 8.4 us)
Async XLA Ops:
  2.7 14.9 %all-to-all-start.2 = ((f32[8,1,1024]{2,1,0:T(1,128)}), f32[8,1,1024]{2,1,0:T(1,128)S(1)}, u32[]{:S(2)}, u32[]{:S(2)}) async-start(f32[8,1,1024]{2,1,0:T(1,128)} %reshape.302), calls=%async_computation.2 | async-start | bytes 65536 | tf_op jit(solution)/shard_map/all_to_all | solution.py:118
  12.5 13.6 %copy-start.9 = (f32[128,256]{1,0:T(8,128)}, f32[128,256]{1,0:T(8,128)S(1)}, u32[]{:S(2)}) copy-start(f32[128,256]{1,0:T(8,128)S(1)} %get-tuple-element.31) | copy-start | bytes 393220
  13.4 4.1 %copy-start.11 = (s32[256]{0:T(256)S(1)}, s32[256]{0:T(256)}, u32[]{:S(2)}) copy-start(s32[256]{0:T(256)} %param.11) | copy-start | bytes 3076
  17.6 12.7 %all-to-all-start = ((f32[8,1,1024]{2,1,0:T(1,128)}), f32[8,1,1024]{2,1,0:T(1,128)S(1)}, u32[]{:S(2)}, u32[]{:S(2)}) async-start(f32[8,1,1024]{2,1,0:T(1,128)} %reshape.300), calls=%async_computation | async-start | bytes 65536 | tf_op jit(solution)/shard_map/all_to_all | solution.py:118
  31.3 3.5 %copy-start.2 = (f32[128,128,1]{1,0,2:T(8,128)S(1)}, f32[128,128,1]{1,0,2:T(8,128)}, u32[]{:S(2)}) copy-start(f32[128,128,1]{1,0,2:T(8,128)} %constant.101) | copy-start | bytes 196612
  34.9 1.2 %copy-start = (f32[16,128,128]{2,1,0:T(8,128)S(1)}, f32[16,128,128]{2,1,0:T(8,128)}, u32[]{:S(2)}) copy-start(f32[16,128,128]{2,1,0:T(8,128)} %param.10) | copy-start | bytes 3145732
  34.9 1.2 %copy-start.7 = (f32[128,128,1]{1,0,2:T(8,128)S(1)}, f32[128,128,1]{1,0,2:T(8,128)}, u32[]{:S(2)}) copy-start(f32[128,128,1]{1,0,2:T(8,128)} %constant.103) | copy-start | bytes 196612
  36.1 0.8 copy-start.1
  39.8 0.8 copy-start.8
  44.4 0.9 copy-start.10
  47.0 25.4 %copy-start.3 = (f32[2,2,128,128]{3,2,1,0:T(8,128)S(1)}, f32[2,2,128,128]{3,2,1,0:T(8,128)}, u32[]{:S(2)}) copy-start(f32[2,2,128,128]{3,2,1,0:T(8,128)} %constant.90.clone) | copy-start | bytes 786436
  47.2 33.7 %copy-start.6 = (bf16[2,64,32,128]{3,2,1,0:T(8,128)(2,1)S(1)}, bf16[2,64,32,128]{3,2,1,0:T(8,128)(2,1)}, u32[]{:S(2)}) copy-start(bf16[2,64,32,128]{3,2,1,0:T(8,128)(2,1)} %get-tuple-element.18) | copy-start | bytes 3145732
  48.1 10.0 %all-to-all-start.1 = ((f32[8,1,1024]{2,1,0:T(1,128)}), f32[8,1,1024]{2,1,0:T(1,128)S(1)}, u32[]{:S(2)}, u32[]{:S(2)}) async-start(f32[8,1,1024]{2,1,0:T(1,128)} %reshape.306), calls=%async_computation.1 | async-start | bytes 65536 | tf_op jit(solution)/shard_map/all_to_all | solution.py:127
  58.1 10.7 %all-to-all-start.3 = ((f32[8,1,1024]{2,1,0:T(1,128)}), f32[8,1,1024]{2,1,0:T(1,128)}, u32[]{:S(2)}, u32[]{:S(2)}) async-start(f32[8,1,1024]{2,1,0:T(1,128)} %reshape.304), calls=%async_computation.3 | async-start | bytes 65536 | tf_op jit(solution)/shard_map/all_to_all | solution.py:127
  62.1 19.2 %copy-start.5 = (bf16[2,64,32,128]{3,2,1,0:T(8,128)(2,1)S(1)}, bf16[2,64,32,128]{3,2,1,0:T(8,128)(2,1)}, u32[]{:S(2)}) copy-start(bf16[2,64,32,128]{3,2,1,0:T(8,128)(2,1)} %get-tuple-element.20) | copy-start | bytes 3145732
  80.8 1.2 %copy-start.4 = (bf16[2,64,32,128]{3,2,1,0:T(8,128)(2,1)S(1)}, bf16[2,64,32,128]{3,2,1,0:T(8,128)(2,1)}, u32[]{:S(2)}) copy-start(bf16[2,64,32,128]{3,2,1,0:T(8,128)(2,1)} %get-tuple-element.19) | copy-start | bytes 3145732
  83.6 9.8 %all-to-all-start.4 = ((f32[2,8,1,256]{3,0,2,1:T(2,128)}), f32[2,8,1,256]{3,0,2,1:T(2,128)S(1)}, u32[]{:S(2)}, u32[]{:S(2)}) async-start(f32[2,8,1,256]{3,0,2,1:T(2,128)} %copy.90), calls=%async_computation.4 | async-start | bytes 32768 | tf_op jit(solution)/shard_map/all_to_all | solution.py:98
where the time goes:
time: 95.2 us; the launch traced here: 94 us
  starting transfers between devices  23.9 us (25%)
  matrix products  22 us (23%)
  waiting for transfers between devices  18.4 us (19%)
  local copies, waits for them, and re-layouts  15.8 us (17%)
  other arithmetic  7.35 us (8%)
  blocking collectives  5.43 us (6%)
  between operations  1.15 us (1%)
    dot_general x20, matrix products, mult(): jnp.dot(left, right, precision=lax.Precision.HIGH, preferred_element_type...  15.8 us
    all_to_all x2, starting transfers between devices, per_device_rows(): lax.all_to_all(z_lines, 'pw', split_axis=0, concat_axis=0, tiled=True)  13.3 us
    all_to_all x2, waiting for transfers between devices, per_device_rows(): lax.all_to_all(outgoing, 'pw', split_axis=0, concat_axis=0, tiled=True)  9.14 us
    all_to_all x2, starting transfers between devices, per_device_rows(): lax.all_to_all(outgoing, 'pw', split_axis=0, concat_axis=0, tiled=True)  7.3 us
    unnamed x33, local copies, waits for them, and re-layouts  7.24 us
    all_to_all x1, waiting for transfers between devices, intersect(): lax.all_to_all(pieces, 'pw', split_axis=1, concat_axis=1, tiled=True)  5.88 us
    all_gather x1, blocking collectives, per_device_rows(): gathered = lax.all_gather(lowered, 'band', axis=1, tiled=True)  5.43 us
    slice x1, local copies, waits for them, and re-layouts, intersect(): psi_all[:, k * width:(k + 1) * width]  4.12 us
  transfers between devices with their start and end apart: 5, of which 4 were waited for; matrix products, arithmetic and copies ran while one was open for 17% of the time, Pallas kernels for 0%

commit v1 on v0

--- a/solution.py
+++ b/solution.py
@@ -1,9 +1,44 @@
+import functools
 import math
 import jax
 import numpy as np
 import jax.numpy as jnp
 from jax import lax
 from jax.sharding import PartitionSpec as P
+
+
+def part_lane(inputs, at_axis, matrix):
+    reply, local_part = (inputs.shape[:at_axis], inputs.shape[at_axis + 1 :])
+    view_out = jnp.moveaxis(inputs.reshape(*reply, matrix, -1, *local_part), at_axis, 0)
+    return view_out
+
+
+def divide_the_panel(x_local, axis_k):
+    x_local = jnp.moveaxis(x_local, 0, axis_k)
+    seen_now = x_local.shape
+    odd = x_local.reshape(
+        *seen_now[:axis_k], seen_now[axis_k] * seen_now[axis_k + 1], *seen_now[axis_k + 2 :]
+    )
+    return odd
+
+
+def lift_task(local, bus_axis, frame_in, m):
+    arr_out, state_next = (lax.axis_size(bus_axis), lax.axis_index(bus_axis))
+    res = part_lane(local, frame_in, arr_out)
+    heap = [res[state_next]]
+    rr = 1
+    while rr < arr_out:
+        formed = res[state_next ^ rr]
+        heap.append(
+            lax.ppermute(formed, axis_name=bus_axis, perm=[(ii, ii ^ rr) for ii in range(arr_out)])
+        )
+        rr = rr + 1
+    res = jnp.stack(heap, 0)[state_next ^ jnp.arange(arr_out)]
+    val = divide_the_panel(res, m)
+    return val
+
+
+load_the_sums_all = functools.partial(lift_task, bus_axis="pw", frame_in=0, m=0)
 
 
 def frequency(index, size):
@@ -115,7 +150,7 @@
     for band in range(psi_block.shape[1]):
         coeffs = psi_block[:, band : band + 1]
         z_lines = jnp.einsum("dczk,cbsk->zdbs", inverse, coeffs, precision=fast)
-        received = lax.all_to_all(z_lines, "pw", split_axis=0, concat_axis=0, tiled=True)
+        received = load_the_sums_all(z_lines)
         lanes = received.shape[1:]
         received = received.reshape((pw_count, planes) + lanes)
         amp = jnp.transpose(received, (2, 3, 1, 0, 4)).reshape(

time: 95.2 us -> 110 us (1.16)
  starting transfers between devices: 23.9 us -> 33.8 us
  local copies, waits for them, and re-layouts: 15.8 us -> 20.2 us
    ppermute x0 -> x14, starting transfers between devices: none -> 23.2 us  [lift_task(): lax.ppermute(formed, axis_name=bus_axis, perm=[(ii, ii ^ rr) for ii in ra...]
    all_to_all x2 -> x0, starting transfers between devices: 13.3 us -> none  [per_device_rows(): lax.all_to_all(z_lines, 'pw', split_axis=0, concat_axis=0, tiled=True)]
    ppermute x0 -> x14, waiting for transfers between devices: none -> 4.28 us  [lift_task(): lax.ppermute(formed, axis_name=bus_axis, perm=[(ii, ii ^ rr) for ii in ra...]
    all_to_all x2 -> x0, waiting for transfers between devices: 3.41 us -> none  [per_device_rows(): lax.all_to_all(z_lines, 'pw', split_axis=0, concat_axis=0, tiled=True)]
    unnamed x33 -> x51, local copies, waits for them, and re-layouts: 7.24 us -> 9.81 us
    all_to_all x2 -> x0, other arithmetic: 1.44 us -> none  [per_device_rows(): lax.all_to_all(z_lines, 'pw', split_axis=0, concat_axis=0, tiled=True)]
    gather x0 -> x2, local copies, waits for them, and re-layouts: none -> 1.11 us  [lift_task(): res = jnp.stack(heap, 0)[state_next ^ jnp.arange(arr_out)]]
  transfers between devices with their start and end apart: 5 -> 17, of which waited for: 4 -> 5; matrix products, arithmetic and copies ran while one was open for 17% -> 19% of each run, Pallas kernels for 0% -> 0%
where the time goes in v1:
time: 110 us; the launch traced here: 109 us
  starting transfers between devices  33.8 us (31%)
  matrix products  22.7 us (21%)
  local copies, waits for them, and re-layouts  20.2 us (18%)
  waiting for transfers between devices  18.9 us (17%)
  other arithmetic  6.91 us (6%)
  blocking collectives  5.43 us (5%)
  between operations  1.29 us (1%)
    ppermute x14, starting transfers between devices, lift_task(): lax.ppermute(formed, axis_name=bus_axis, perm=[(ii, ii ^ rr) for ii in ra...  23.2 us
    dot_general x20, matrix products, mult(): jnp.dot(left, right, precision=lax.Precision.HIGH, preferred_element_type...  16.5 us
    unnamed x51, local copies, waits for them, and re-layouts  9.81 us
    all_to_all x2, waiting for transfers between devices, per_device_rows(): lax.all_to_all(outgoing, 'pw', split_axis=0, concat_axis=0, tiled=True)  8.7 us
    all_to_all x2, starting transfers between devices, per_device_rows(): lax.all_to_all(outgoing, 'pw', split_axis=0, concat_axis=0, tiled=True)  7.28 us
    all_to_all x1, waiting for transfers between devices, intersect(): lax.all_to_all(pieces, 'pw', split_axis=1, concat_axis=1, tiled=True)  5.88 us
    all_gather x1, blocking collectives, per_device_rows(): gathered = lax.all_gather(lowered, 'band', axis=1, tiled=True)  5.43 us
    ppermute x14, waiting for transfers between devices, lift_task(): lax.ppermute(formed, axis_name=bus_axis, perm=[(ii, ii ^ rr) for ii in ra...  4.28 us
  transfers between devices with their start and end apart: 17, of which 5 were waited for; matrix products, arithmetic and copies ran while one was open for 19% of the time, Pallas kernels for 0%

profile of v1, /device:TPU:0, one launch (start us, length us, event | category | flops | bytes accessed | tf_op | source)
XLA Modules:
  0.0 109.1 jit_solution(5192806930592682557)
XLA Ops:
  0.7 1.2 %convolution_bitcast_fusion.1 = f32[128,2,1,32]{0,3,1,2:T(8,128)S(1)} fusion(f32[2,2,128,128]{3,2,1,0:T(8,128)} %constant.105.clone, f32[2,2,32,128]{3,2,1,0:T(8,128)} %param.8), kind=kOutput, calls=%fused_computation.35 | convolution fusion | flops 12582912 | bytes 327680 | tf_op jit(solution)/shard_map/dczk,cbsk->zdbs/dot_general | solution.py:152
  2.1 3.0 %collective-permute-start.7 = (f32[16,2,1,32]{3,0,1,2:T(8,128)S(1)}, f32[16,2,1,32]{3,0,1,2:T(8,128)S(1)}, u32[]{:S(2)}, u32[]{:S(2)}) collective-permute-start(f32[16,2,1,32]{3,0,1,2:T(8,128)S(1)} %get-tuple-element.32), channel_id=1, source_target_pairs={{0,4},{4,0},{8,12},{12,8},{16,20},{20,16},{24,28},{28,24},{1,5},{5... | collective-permute-start | bytes 12296 | tf_op jit(solution)/shard_map/ppermute | solution.py:33
  5.1 1.6 %collective-permute-start.8 = (f32[16,2,1,32]{3,0,1,2:T(8,128)S(1)}, f32[16,2,1,32]{3,0,1,2:T(8,128)S(1)}, u32[]{:S(2)}, u32[]{:S(2)}) collective-permute-start(f32[16,2,1,32]{3,0,1,2:T(8,128)S(1)} %get-tuple-element.31), channel_id=1, source_target_pairs={{0,8},{4,12},{8,0},{12,4},{16,24},{20,28},{24,16},{28,20},{1,9},{5... | collective-permute-start | bytes 12296 | tf_op jit(solution)/shard_map/ppermute | solution.py:33
  6.7 3.0 %collective-permute-start.10 = (f32[16,2,1,32]{3,0,1,2:T(8,128)S(1)}, f32[16,2,1,32]{3,0,1,2:T(8,128)S(1)}, u32[]{:S(2)}, u32[]{:S(2)}) collective-permute-start(f32[16,2,1,32]{3,0,1,2:T(8,128)S(1)} %get-tuple-element.29), channel_id=1, source_target_pairs={{0,16},{4,20},{8,24},{12,28},{16,0},{20,4},{24,8},{28,12},{1,17},{... | collective-permute-start | bytes 12296 | tf_op jit(solution)/shard_map/ppermute | solution.py:33
  9.6 1.3 %collective-permute-start.11 = (f32[16,2,1,32]{3,0,1,2:T(8,128)S(1)}, f32[16,2,1,32]{3,0,1,2:T(8,128)S(1)}, u32[]{:S(2)}, u32[]{:S(2)}) collective-permute-start(f32[16,2,1,32]{3,0,1,2:T(8,128)S(1)} %get-tuple-element.28), channel_id=1, source_target_pairs={{0,20},{4,16},{8,28},{12,24},{16,4},{20,0},{24,12},{28,8},{1,21},{... | collective-permute-start | bytes 12296 | tf_op jit(solution)/shard_map/ppermute | solution.py:33
  10.9 1.2 %convolution_bitcast_fusion.3 = f32[128,2,1,32]{0,3,1,2:T(8,128)S(1)} fusion(f32[2,2,128,128]{3,2,1,0:T(8,128)} %constant.105.clone, f32[2,2,32,128]{3,2,1,0:T(8,128)} %param.8), kind=kOutput, calls=%fused_computation.37 | convolution fusion | flops 12582912 | bytes 327680 | tf_op jit(solution)/shard_map/dczk,cbsk->zdbs/dot_general | solution.py:152
  13.5 0.7 and_select_fusion
  14.7 4.2 %fusion.89 = (bf16[2,64,32,128]{3,2,1,0:T(8,128)(2,1)}, bf16[2,64,32,128]{3,2,1,0:T(8,128)(2,1)}, bf16[2,64,32,128]{3,2,1,0:T(8,128)(2,1)}, bf16[2,64,32,128]{3,2,1,0:T(8,128)(2,1)S(1)}) fusion(bf16[2,256,32,128]{3,2,1,0:T(8,128)(2,1)} %param.9), kind=kLoop, calls=%fused_computation.164 | loop fusion | bytes 8388608 | tf_op jit(solution)/shard_map/slice | solution.py:120
  18.9 0.7 fusion.82
  19.5 3.6 %collective-permute-start.12 = (f32[16,2,1,32]{3,0,1,2:T(8,128)S(1)}, f32[16,2,1,32]{3,0,1,2:T(8,128)S(1)}, u32[]{:S(2)}, u32[]{:S(2)}) collective-permute-start(f32[16,2,1,32]{3,0,1,2:T(8,128)S(1)} %get-tuple-element.27), channel_id=1, source_target_pairs={{0,24},{4,28},{8,16},{12,20},{16,8},{20,12},{24,0},{28,4},{1,25},{... | collective-permute-start | bytes 12296 | tf_op jit(solution)/shard_map/ppermute | solution.py:33
  23.2 1.7 %collective-permute-start = (f32[16,2,1,32]{3,0,1,2:T(8,128)}, f32[16,2,1,32]{3,0,1,2:T(8,128)}, u32[]{:S(2)}, u32[]{:S(2)}) collective-permute-start(f32[16,2,1,32]{3,0,1,2:T(8,128)} %get-tuple-element.41), channel_id=1, source_target_pairs={{0,4},{4,0},{8,12},{12,8},{16,20},{20,16},{24,28},{28,24},{1,5},{5... | collective-permute-start | bytes 12296 | tf_op jit(solution)/shard_map/ppermute | solution.py:33
  24.9 1.9 %collective-permute-start.2 = (f32[16,2,1,32]{3,0,1,2:T(8,128)}, f32[16,2,1,32]{3,0,1,2:T(8,128)}, u32[]{:S(2)}, u32[]{:S(2)}) collective-permute-start(f32[16,2,1,32]{3,0,1,2:T(8,128)} %get-tuple-element.39), channel_id=1, source_target_pairs={{0,12},{4,8},{8,4},{12,0},{16,28},{20,24},{24,20},{28,16},{1,13},{... | collective-permute-start | bytes 12296 | tf_op jit(solution)/shard_map/ppermute | solution.py:33
  26.7 2.4 %collective-permute-start.3 = (f32[16,2,1,32]{3,0,1,2:T(8,128)}, f32[16,2,1,32]{3,0,1,2:T(8,128)}, u32[]{:S(2)}, u32[]{:S(2)}) collective-permute-start(f32[16,2,1,32]{3,0,1,2:T(8,128)} %get-tuple-element.38), channel_id=1, source_target_pairs={{0,16},{4,20},{8,24},{12,28},{16,0},{20,4},{24,8},{28,12},{1,17},{... | collective-permute-start | bytes 12296 | tf_op jit(solution)/shard_map/ppermute | solution.py:33
  29.7 1.0 collective-permute-start.4
  32.1 0.8 fusion
  32.9 1.5 %fusion.4 = f32[16,128,128]{2,1,0:T(8,128)S(1)} fusion(f32[16,256]{1,0:T(8,128)} %copy-done.12, f32[16,256]{1,0:T(8,128)} %copy-done.11, f32[128,256]{1,0:T(8,128)S(1)} %get-tuple-element.45, f32[128,256]{1,0:T(8,128)S(1)} %get-tuple-element.44, s32[256]{0:T(256)S(1)} %get-tuple-element.42), kind=kOutput, calls=%fused_computation.8 | convolution fusion | flops 404258816 | bytes 1344512 | tf_op jit(solution)/shard_map/dot_general | solution.py:82
  34.5 3.7 %collective-permute-start.5 = (f32[16,2,1,32]{3,0,1,2:T(8,128)}, f32[16,2,1,32]{3,0,1,2:T(8,128)S(1)}, u32[]{:S(2)}, u32[]{:S(2)}) collective-permute-start(f32[16,2,1,32]{3,0,1,2:T(8,128)} %get-tuple-element.36), channel_id=1, source_target_pairs={{0,24},{4,28},{8,16},{12,20},{16,8},{20,12},{24,0},{28,4},{1,25},{... | collective-permute-start | bytes 12296 | tf_op jit(solution)/shard_map/ppermute | solution.py:33
  38.2 0.7 constant_dynamic-update-slice_fusion.6
  39.0 0.7 constant_dynamic-update-slice_fusion.5
  39.7 0.7 constant_dynamic-update-slice_fusion.4
  40.4 0.7 constant_dynamic-update-slice_fusion.3
  41.1 0.7 constant_dynamic-update-slice_fusion.2
  41.9 3.7 %collective-permute-done.6 = f32[16,2,1,32]{3,0,1,2:T(8,128)S(1)} collective-permute-done((f32[16,2,1,32]{3,0,1,2:T(8,128)}, f32[16,2,1,32]{3,0,1,2:T(8,128)S(1)}, u32[]{:S(2)}, u32[]{:S(2)}) %collective-permute-start.6) | collective-permute-done | bytes 4128 | tf_op jit(solution)/shard_map/ppermute | solution.py:33
  46.4 1.7 %fusion.8 = f32[16,128,128]{2,1,0:T(8,128)S(1)} fusion(f32[128,256]{1,0:T(8,128)} %copy-done.9, f32[16,256]{1,0:T(8,128)S(1)} %mul.266, f32[128,256]{1,0:T(8,128)S(1)} %get-tuple-element.44, f32[16,256]{1,0:T(8,128)S(1)} %mul.257, s32[256]{0:T(256)S(1)} %get-tuple-element.42), kind=kOutput, calls=%fused_computation.14 | convolution fusion | flops 404258816 | bytes 1344512 | tf_op jit(solution)/shard_map/dot_general | solution.py:82
  48.1 1.7 %fusion.12 = f32[16,128,128]{2,1,0:T(8,128)S(1)} fusion(f32[128,256]{1,0:T(8,128)} %copy-done.9, f32[16,256]{1,0:T(8,128)S(1)} %mul.266, f32[128,256]{1,0:T(8,128)S(1)} %get-tuple-element.44, f32[16,256]{1,0:T(8,128)S(1)} %mul.257, s32[256]{0:T(256)S(1)} %get-tuple-element.42), kind=kOutput, calls=%fused_computation.18 | convolution fusion | flops 404258816 | bytes 1344512 | tf_op jit(solution)/shard_map/dot_general | solution.py:82
  56.7 0.8 convolution_subtract_fusion.3
  58.1 0.7 fusion.60
  58.8 0.7 fusion.62
  59.5 0.7 fusion.66
  60.4 1.6 %add_reduce_fusion.1 = (f32[16,256]{1,0:T(8,128)S(1)}, f32[16,256]{1,0:T(8,128)S(1)}, f32[16,256]{1,0:T(8,128)S(1)}, f32[16,256]{1,0:T(8,128)S(1)}) fusion(f32[16,128,256]{2,1,0:T(8,128)S(1)} %fusion.66, f32[128,256]{1,0:T(8,128)S(1)} %copy-done.10, f32[128,256]{1,0:T(8,128)S(1)} %get-tuple-element.44, f32[16,128,256]{2,1,0:T(8,128)S(1)} %fusion.62, ...), kind=kOutput, calls=%fused_computation.13 | convolution fusion | flops 411058176 | bytes 7668736 | tf_op jit(solution)/shard_map/dot_general | solution.py:82
  62.4 0.8 reshape.338
  63.2 3.3 %all-to-all-start = ((f32[8,1,1024]{2,1,0:T(1,128)}), f32[8,1,1024]{2,1,0:T(1,128)S(1)}, u32[]{:S(2)}, u32[]{:S(2)}) async-start(f32[8,1,1024]{2,1,0:T(1,128)} %reshape.338), calls=%async_computation | async-start | bytes 65536 | tf_op jit(solution)/shard_map/all_to_all | solution.py:162
  66.9 0.8 reshape.336
  67.6 5.5 %all-to-all-done = f32[8,1,1024]{2,1,0:T(1,128)S(1)} async-done(((f32[8,1,1024]{2,1,0:T(1,128)}), f32[8,1,1024]{2,1,0:T(1,128)S(1)}, u32[]{:S(2)}, u32[]{:S(2)}) %all-to-all-start) | async-done | bytes 32800 | tf_op jit(solution)/shard_map/all_to_all | solution.py:162
  73.2 4.0 %all-to-all-start.1 = ((f32[8,1,1024]{2,1,0:T(1,128)}), f32[8,1,1024]{2,1,0:T(1,128)}, u32[]{:S(2)}, u32[]{:S(2)}) async-start(f32[8,1,1024]{2,1,0:T(1,128)} %reshape.336), calls=%async_computation.1 | async-start | bytes 65536 | tf_op jit(solution)/shard_map/all_to_all | solution.py:162
  77.7 1.3 %reduce.10 = f32[8,1024]{1,0:T(8,128)} reduce(f32[8,1,1024]{2,1,0:T(1,128)S(1)} %all-to-all-done, f32[]{:T(128)} %broadcast.293), dimensions={1}, to_apply=%all_to_all.9.reduce_sub_computation | reduce | bytes 65540 | tf_op jit(solution)/shard_map/all_to_all | solution.py:162
  79.0 0.9 reshape.339
  80.0 0.7 copy.78
  80.6 3.2 %all-to-all-done.1 = f32[8,1,1024]{2,1,0:T(1,128)} async-done(((f32[8,1,1024]{2,1,0:T(1,128)}), f32[8,1,1024]{2,1,0:T(1,128)}, u32[]{:S(2)}, u32[]{:S(2)}) %all-to-all-start.1) | async-done | bytes 32800 | tf_op jit(solution)/shard_map/all_to_all | solution.py:162
  83.8 2.1 %reduce.9 = f32[8,1024]{1,0:T(8,128)} reduce(f32[8,1,1024]{2,1,0:T(1,128)} %all-to-all-done.1, f32[]{:T(128)} %broadcast.293), dimensions={1}, to_apply=%all_to_all.10.reduce_sub_computation | reduce | bytes 65540 | tf_op jit(solution)/shard_map/all_to_all | solution.py:162
  85.9 0.9 reshape.337
  86.8 0.7 copy.86
  87.5 1.0 convolution_bitcast_fusion.2
  88.6 1.0 convolution_bitcast_fusion
  89.6 0.9 fusion.88
  90.5 5.4 %all_gather.3 = bf16[2,8,32,128]{3,2,0,1:T(8,128)(2,1)S(1)} all-gather(bf16[2,2,32,128]{3,2,0,1:T(8,128)(2,1)S(1)} %get-tuple-element.16), channel_id=1, replica_groups=mesh['pw'=8,'band'=4] {'band'}, dimensions={1}, use_global_device_ids=true | all-gather | bytes 163840 | tf_op jit(solution)/shard_map/all_gather | solution.py:167
  98.7 3.3 %all-to-all-start.2 = ((f32[2,8,1,256]{3,0,2,1:T(2,128)}), f32[2,8,1,256]{3,0,2,1:T(2,128)S(1)}, u32[]{:S(2)}, u32[]{:S(2)}) async-start(f32[2,8,1,256]{3,0,2,1:T(2,128)} %copy.94), calls=%async_computation.2 | async-start | bytes 32768 | tf_op jit(solution)/shard_map/all_to_all | solution.py:133
  102.6 5.9 %all-to-all-done.2 = f32[2,8,1,256]{3,0,2,1:T(2,128)S(1)} async-done(((f32[2,8,1,256]{3,0,2,1:T(2,128)}), f32[2,8,1,256]{3,0,2,1:T(2,128)S(1)}, u32[]{:S(2)}, u32[]{:S(2)}) %all-to-all-start.2) | async-done | bytes 16416 | tf_op jit(solution)/shard_map/all_to_all | solution.py:133
  (114 shorter events, 17.7 us)
Async XLA Ops:
  2.1 17.5 %collective-permute-start.7 = (f32[16,2,1,32]{3,0,1,2:T(8,128)S(1)}, f32[16,2,1,32]{3,0,1,2:T(8,128)S(1)}, u32[]{:S(2)}, u32[]{:S(2)}) collective-permute-start(f32[16,2,1,32]{3,0,1,2:T(8,128)S(1)} %get-tuple-element.32), channel_id=1, source_target_pairs={{0,4},{4,0},{8,12},{12,8},{16,20},{20,16},{24,28},{28,24},{1,5},{5... | collective-permute-start | bytes 12296 | tf_op jit(solution)/shard_map/ppermute | solution.py:33
  5.1 18.1 %collective-permute-start.8 = (f32[16,2,1,32]{3,0,1,2:T(8,128)S(1)}, f32[16,2,1,32]{3,0,1,2:T(8,128)S(1)}, u32[]{:S(2)}, u32[]{:S(2)}) collective-permute-start(f32[16,2,1,32]{3,0,1,2:T(8,128)S(1)} %get-tuple-element.31), channel_id=1, source_target_pairs={{0,8},{4,12},{8,0},{12,4},{16,24},{20,28},{24,16},{28,20},{1,9},{5... | collective-permute-start | bytes 12296 | tf_op jit(solution)/shard_map/ppermute | solution.py:33
  6.7 16.5 %collective-permute-start.9 = (f32[16,2,1,32]{3,0,1,2:T(8,128)S(1)}, f32[16,2,1,32]{3,0,1,2:T(8,128)S(1)}, u32[]{:S(2)}, u32[]{:S(2)}) collective-permute-start(f32[16,2,1,32]{3,0,1,2:T(8,128)S(1)} %get-tuple-element.30), channel_id=1, source_target_pairs={{0,12},{4,8},{8,4},{12,0},{16,28},{20,24},{24,20},{28,16},{1,13},{... | collective-permute-start | bytes 12296 | tf_op jit(solution)/shard_map/ppermute | solution.py:33
  6.7 18.2 %collective-permute-start.10 = (f32[16,2,1,32]{3,0,1,2:T(8,128)S(1)}, f32[16,2,1,32]{3,0,1,2:T(8,128)S(1)}, u32[]{:S(2)}, u32[]{:S(2)}) collective-permute-start(f32[16,2,1,32]{3,0,1,2:T(8,128)S(1)} %get-tuple-element.29), channel_id=1, source_target_pairs={{0,16},{4,20},{8,24},{12,28},{16,0},{20,4},{24,8},{28,12},{1,17},{... | collective-permute-start | bytes 12296 | tf_op jit(solution)/shard_map/ppermute | solution.py:33
  9.6 15.2 %collective-permute-start.11 = (f32[16,2,1,32]{3,0,1,2:T(8,128)S(1)}, f32[16,2,1,32]{3,0,1,2:T(8,128)S(1)}, u32[]{:S(2)}, u32[]{:S(2)}) collective-permute-start(f32[16,2,1,32]{3,0,1,2:T(8,128)S(1)} %get-tuple-element.28), channel_id=1, source_target_pairs={{0,20},{4,16},{8,28},{12,24},{16,4},{20,0},{24,12},{28,8},{1,21},{... | collective-permute-start | bytes 12296 | tf_op jit(solution)/shard_map/ppermute | solution.py:33
  14.7 18.3 %copy-start.9 = (f32[128,256]{1,0:T(8,128)}, f32[128,256]{1,0:T(8,128)S(1)}, u32[]{:S(2)}) copy-start(f32[128,256]{1,0:T(8,128)S(1)} %get-tuple-element.45) | copy-start | bytes 393220
  14.7 4.2 %copy-start.13 = (s32[256]{0:T(256)S(1)}, s32[256]{0:T(256)}, u32[]{:S(2)}) copy-start(s32[256]{0:T(256)} %param.11) | copy-start | bytes 3076
  19.5 7.2 %collective-permute-start.12 = (f32[16,2,1,32]{3,0,1,2:T(8,128)S(1)}, f32[16,2,1,32]{3,0,1,2:T(8,128)S(1)}, u32[]{:S(2)}, u32[]{:S(2)}) collective-permute-start(f32[16,2,1,32]{3,0,1,2:T(8,128)S(1)} %get-tuple-element.27), channel_id=1, source_target_pairs={{0,24},{4,28},{8,16},{12,20},{16,8},{20,12},{24,0},{28,4},{1,25},{... | collective-permute-start | bytes 12296 | tf_op jit(solution)/shard_map/ppermute | solution.py:33
  23.1 6.5 %collective-permute-start.13 = (f32[16,2,1,32]{3,0,1,2:T(8,128)S(1)}, f32[16,2,1,32]{3,0,1,2:T(8,128)S(1)}, u32[]{:S(2)}, u32[]{:S(2)}) collective-permute-start(f32[16,2,1,32]{3,0,1,2:T(8,128)S(1)} %get-tuple-element.26), channel_id=1, source_target_pairs={{0,28},{4,24},{8,20},{12,16},{16,12},{20,8},{24,4},{28,0},{1,29},{... | collective-permute-start | bytes 12296 | tf_op jit(solution)/shard_map/ppermute | solution.py:33
  23.2 11.3 %collective-permute-start = (f32[16,2,1,32]{3,0,1,2:T(8,128)}, f32[16,2,1,32]{3,0,1,2:T(8,128)}, u32[]{:S(2)}, u32[]{:S(2)}) collective-permute-start(f32[16,2,1,32]{3,0,1,2:T(8,128)} %get-tuple-element.41), channel_id=1, source_target_pairs={{0,4},{4,0},{8,12},{12,8},{16,20},{20,16},{24,28},{28,24},{1,5},{5... | collective-permute-start | bytes 12296 | tf_op jit(solution)/shard_map/ppermute | solution.py:33
  24.8 14.0 %collective-permute-start.1 = (f32[16,2,1,32]{3,0,1,2:T(8,128)}, f32[16,2,1,32]{3,0,1,2:T(8,128)}, u32[]{:S(2)}, u32[]{:S(2)}) collective-permute-start(f32[16,2,1,32]{3,0,1,2:T(8,128)} %get-tuple-element.40), channel_id=1, source_target_pairs={{0,8},{4,12},{8,0},{12,4},{16,24},{20,28},{24,16},{28,20},{1,9},{5... | collective-permute-start | bytes 12296 | tf_op jit(solution)/shard_map/ppermute | solution.py:33
  24.9 14.8 %collective-permute-start.2 = (f32[16,2,1,32]{3,0,1,2:T(8,128)}, f32[16,2,1,32]{3,0,1,2:T(8,128)}, u32[]{:S(2)}, u32[]{:S(2)}) collective-permute-start(f32[16,2,1,32]{3,0,1,2:T(8,128)} %get-tuple-element.39), channel_id=1, source_target_pairs={{0,12},{4,8},{8,4},{12,0},{16,28},{20,24},{24,20},{28,16},{1,13},{... | collective-permute-start | bytes 12296 | tf_op jit(solution)/shard_map/ppermute | solution.py:33
  26.7 13.7 %collective-permute-start.3 = (f32[16,2,1,32]{3,0,1,2:T(8,128)}, f32[16,2,1,32]{3,0,1,2:T(8,128)}, u32[]{:S(2)}, u32[]{:S(2)}) collective-permute-start(f32[16,2,1,32]{3,0,1,2:T(8,128)} %get-tuple-element.38), channel_id=1, source_target_pairs={{0,16},{4,20},{8,24},{12,28},{16,0},{20,4},{24,8},{28,12},{1,17},{... | collective-permute-start | bytes 12296 | tf_op jit(solution)/shard_map/ppermute | solution.py:33
  29.7 11.4 %collective-permute-start.4 = (f32[16,2,1,32]{3,0,1,2:T(8,128)}, f32[16,2,1,32]{3,0,1,2:T(8,128)}, u32[]{:S(2)}, u32[]{:S(2)}) collective-permute-start(f32[16,2,1,32]{3,0,1,2:T(8,128)} %get-tuple-element.37), channel_id=1, source_target_pairs={{0,20},{4,16},{8,28},{12,24},{16,4},{20,0},{24,12},{28,8},{1,21},{... | collective-permute-start | bytes 12296 | tf_op jit(solution)/shard_map/ppermute | solution.py:33
  31.4 0.6 copy-start.11
  31.5 0.6 copy-start.12
  34.5 7.4 %collective-permute-start.5 = (f32[16,2,1,32]{3,0,1,2:T(8,128)}, f32[16,2,1,32]{3,0,1,2:T(8,128)S(1)}, u32[]{:S(2)}, u32[]{:S(2)}) collective-permute-start(f32[16,2,1,32]{3,0,1,2:T(8,128)} %get-tuple-element.36), channel_id=1, source_target_pairs={{0,24},{4,28},{8,16},{12,20},{16,8},{20,12},{24,0},{28,4},{1,25},{... | collective-permute-start | bytes 12296 | tf_op jit(solution)/shard_map/ppermute | solution.py:33
  38.9 6.6 %collective-permute-start.6 = (f32[16,2,1,32]{3,0,1,2:T(8,128)}, f32[16,2,1,32]{3,0,1,2:T(8,128)S(1)}, u32[]{:S(2)}, u32[]{:S(2)}) collective-permute-start(f32[16,2,1,32]{3,0,1,2:T(8,128)} %get-tuple-element.35), channel_id=1, source_target_pairs={{0,28},{4,24},{8,20},{12,16},{16,12},{20,8},{24,4},{28,0},{1,29},{... | collective-permute-start | bytes 12296 | tf_op jit(solution)/shard_map/ppermute | solution.py:33
  46.2 3.5 %copy-start.2 = (f32[128,128,1]{1,0,2:T(8,128)S(1)}, f32[128,128,1]{1,0,2:T(8,128)}, u32[]{:S(2)}) copy-start(f32[128,128,1]{1,0,2:T(8,128)} %constant.117) | copy-start | bytes 196612
  49.8 1.2 %copy-start = (f32[16,128,128]{2,1,0:T(8,128)S(1)}, f32[16,128,128]{2,1,0:T(8,128)}, u32[]{:S(2)}) copy-start(f32[16,128,128]{2,1,0:T(8,128)} %param.10) | copy-start | bytes 3145732
  49.8 1.2 %copy-start.7 = (f32[128,128,1]{1,0,2:T(8,128)S(1)}, f32[128,128,1]{1,0,2:T(8,128)}, u32[]{:S(2)}) copy-start(f32[128,128,1]{1,0,2:T(8,128)} %constant.119) | copy-start | bytes 196612
  51.0 0.8 copy-start.1
  54.7 0.8 copy-start.8
  59.5 0.9 copy-start.10
  62.1 15.0 %copy-start.14 = (f32[128]{0:T(128)S(1)}, f32[128]{0:T(128)}, u32[]{:S(2)}) copy-start(f32[128]{0:T(128)} %fusion.86) | copy-start | bytes 1540
  62.1 15.0 %copy-start.15 = (f32[32]{0:T(128)S(1)}, f32[32]{0:T(128)}, u32[]{:S(2)}) copy-start(f32[32]{0:T(128)} %fusion.82) | copy-start | bytes 388
  62.1 25.4 %copy-start.3 = (f32[2,2,128,128]{3,2,1,0:T(8,128)S(1)}, f32[2,2,128,128]{3,2,1,0:T(8,128)}, u32[]{:S(2)}) copy-start(f32[2,2,128,128]{3,2,1,0:T(8,128)} %constant.106.clone) | copy-start | bytes 786436
  62.3 33.7 %copy-start.6 = (bf16[2,64,32,128]{3,2,1,0:T(8,128)(2,1)S(1)}, bf16[2,64,32,128]{3,2,1,0:T(8,128)(2,1)}, u32[]{:S(2)}) copy-start(bf16[2,64,32,128]{3,2,1,0:T(8,128)(2,1)} %get-tuple-element.18) | copy-start | bytes 3145732
  63.2 10.0 %all-to-all-start = ((f32[8,1,1024]{2,1,0:T(1,128)}), f32[8,1,1024]{2,1,0:T(1,128)S(1)}, u32[]{:S(2)}, u32[]{:S(2)}) async-start(f32[8,1,1024]{2,1,0:T(1,128)} %reshape.338), calls=%async_computation | async-start | bytes 65536 | tf_op jit(solution)/shard_map/all_to_all | solution.py:162
  73.2 10.7 %all-to-all-start.1 = ((f32[8,1,1024]{2,1,0:T(1,128)}), f32[8,1,1024]{2,1,0:T(1,128)}, u32[]{:S(2)}, u32[]{:S(2)}) async-start(f32[8,1,1024]{2,1,0:T(1,128)} %reshape.336), calls=%async_computation.1 | async-start | bytes 65536 | tf_op jit(solution)/shard_map/all_to_all | solution.py:162
  77.2 19.2 %copy-start.5 = (bf16[2,64,32,128]{3,2,1,0:T(8,128)(2,1)S(1)}, bf16[2,64,32,128]{3,2,1,0:T(8,128)(2,1)}, u32[]{:S(2)}) copy-start(bf16[2,64,32,128]{3,2,1,0:T(8,128)(2,1)} %get-tuple-element.20) | copy-start | bytes 3145732
  95.9 1.2 %copy-start.4 = (bf16[2,64,32,128]{3,2,1,0:T(8,128)(2,1)S(1)}, bf16[2,64,32,128]{3,2,1,0:T(8,128)(2,1)}, u32[]{:S(2)}) copy-start(bf16[2,64,32,128]{3,2,1,0:T(8,128)(2,1)} %get-tuple-element.19) | copy-start | bytes 3145732
  98.7 9.9 %all-to-all-start.2 = ((f32[2,8,1,256]{3,0,2,1:T(2,128)}), f32[2,8,1,256]{3,0,2,1:T(2,128)S(1)}, u32[]{:S(2)}, u32[]{:S(2)}) async-start(f32[2,8,1,256]{3,0,2,1:T(2,128)} %copy.94), calls=%async_computation.2 | async-start | bytes 32768 | tf_op jit(solution)/shard_map/all_to_all | solution.py:133
